TPU v7x, 32 devices: a whole 2x2x4 slice. The times are simulated.
32 devices in a mesh: grp: 2 (over y), row: 4 (over z), col: 2 (over x), vec: 2 (over core).
Axes of the slice: x: 2, y: 2, z: 4, core: 2. Of those that a mesh axis runs over, the one named last changes fastest.
Arguments:
- start: float32 [64, 2048], P('vec', ('grp', 'row')), parts along dimension 1, may hold values from -6 to 6
- tiles: bfloat16 [16, 32, 128, 128], P(('grp', 'row'), 'col'), parts along dimension 0, may hold values from -6 to 6
- pattern: int32 [16, 32], P(('grp', 'row')), parts along dimension 0, may hold values from 0 to 7
- counts: int32 [16], P(('grp', 'row')), parts along dimension 0, may hold values from 1 to 32
Outputs:
- basis: float32 [64, 2048], P('vec', ('grp', 'row')), parts along dimension 1
There are 2 independent parts, one for each index of `grp`. A program takes and returns all parts, laid end to end along the dimension named above; each array names one. Nothing has to cross between parts.
Inputs may be any that keep to these rules, and one draw needn't show every extreme that they name: pattern may name a block column more than once in a block row; such tiles add.
All inputs are finite; a program needn't handle non-finite values.
Results may differ from a plain program's by a relative error of at most 0.03.
Values may be sent and summed in bfloat16 or wider, within the bound.
No kernel may reach another device: no remote copies, remote signals or barrier semaphores. Data moves between devices by JAX's collectives and lax.ppermute only.
A program may use at most 64 MiB of HBM per device.

v0:
```python
import jax
import jax.numpy as jnp
from jax import lax
from jax.sharding import PartitionSpec as P

DEGREE = 8
ITERS = 2
HALF_WIDTH = 2.0
EPSILON = 1e-06


def row_scaling(square_sums, live_counts, block):
    entries = (live_counts * block).astype(jnp.float32)[:, None]
    scaled = lax.rsqrt(square_sums / entries + EPSILON) / jnp.sqrt(entries)
    return (scaled / HALF_WIDTH).reshape(1, -1)


def chebyshev(first, apply):
    previous = first
    present = apply(first)
    for step in range(DEGREE - 1):
        previous, present = (present, 2.0 * apply(present) - previous)
    return present


def orthonormal(mine, total_rows):
    both = lax.all_gather(mine.astype(jnp.bfloat16), "vec", axis=0, tiled=True).astype(mine.dtype)
    part_gram = jnp.dot(both, both.T, precision=lax.Precision.HIGHEST)
    gram = lax.psum(part_gram, "row") / total_rows
    lower = jnp.linalg.cholesky(gram)
    solved = jax.scipy.linalg.solve_triangular(lower, both, lower=True)
    width = mine.shape[0]
    return lax.dynamic_slice_in_dim(solved, lax.axis_index("vec") * width, width, 0)


def per_device(start, tiles, pattern, counts):
    nb_dev = tiles.shape[0]
    block = tiles.shape[2]
    total_rows = nb_dev * block * lax.axis_size("row")
    vec_cols = start.shape[0]
    col_index = lax.axis_index("col")
    kb_dev = tiles.shape[1]
    slot_ids = col_index * kb_dev + jnp.arange(kb_dev, dtype=jnp.int32)
    live = (slot_ids[None, :] < counts[:, None]).astype(jnp.bfloat16)
    masked = tiles * live[:, :, None, None]
    local_pattern = lax.dynamic_slice_in_dim(pattern, col_index * kb_dev, kb_dev, 1)
    partial_squares = jnp.einsum(
        "bkmn,bkmn->bm", masked, masked, preferred_element_type=jnp.float32
    )
    square_sums = lax.psum(partial_squares, "col")
    scaling = row_scaling(square_sums, counts, block)

    def apply_slots(current):
        whole = lax.all_gather(current.astype(jnp.bfloat16), "row", axis=1, tiled=True)
        blocks = whole.reshape(vec_cols, -1, block)
        picked = jnp.take(blocks, local_pattern, axis=1)
        product = jnp.einsum("cbkn,bkmn->cbm", picked, masked, preferred_element_type=jnp.float32)
        total = lax.psum(product.astype(jnp.bfloat16), "col").astype(jnp.float32)
        return total.reshape(vec_cols, -1) * scaling

    current = start
    for outer in range(ITERS):
        filtered = chebyshev(current, apply_slots)
        current = orthonormal(filtered, total_rows)
    return current


def solution(mesh):
    in_specs = (
        P("vec", ("grp", "row")),
        P(("grp", "row"), "col", None, None),
        P(("grp", "row"), None),
        P(("grp", "row")),
    )
    out_specs = P("vec", ("grp", "row"))
    return jax.shard_map(
        per_device, mesh=mesh, in_specs=in_specs, out_specs=out_specs, check_vma=False
    )
```

profile of v0, /device:TPU:0, one launch (start us, length us, event | category | flops | bytes accessed | tf_op | source)
XLA Modules:
  0.0 427.7 jit_solution(17464882422868183498)
XLA Ops:
  0.0 0.8 compare_convert_fusion
  0.8 0.7 fusion.135
  1.5 0.7 multiply_convert_fusion
  2.2 1.6 fusion
  3.8 5.8 %psum.134 = f32[2,128]{1,0:T(2,128)S(1)} all-reduce(f32[2,128]{1,0:T(2,128)S(1)} %fusion), channel_id=1, replica_groups=mesh['grp'=2,'row'=4,'col'=2,'vec'=2] {'col'}, use_global_device_ids=true, to_apply=%region_1.0 | all-reduce | flops 256 | bytes 2048 | tf_op jit(solution)/shard_map/psum | solution.py:50
  9.9 14.0 %all_gather.54 = bf16[32,1024]{1,0:T(8,128)(2,1)S(1)} all-gather(bf16[32,256]{1,0:T(8,128)(2,1)S(1)} %convert_element_type.183), channel_id=1, replica_groups=mesh['grp'=2,'row'=4,'col'=2,'vec'=2] {'row'}, dimensions={1}, use_global_device_ids=true | all-gather | bytes 81920 | tf_op jit(solution)/shard_map/all_gather | solution.py:54
  23.9 0.6 gather_fusion
  25.1 8.2 %psum.133 = bf16[32,256]{1,0:T(8,128)(2,1)S(1)} all-reduce(bf16[32,256]{1,0:T(8,128)(2,1)S(1)} %bitcast.395), channel_id=1, replica_groups=mesh['grp'=2,'row'=4,'col'=2,'vec'=2] {'col'}, use_global_device_ids=true, to_apply=%region_0.2 | all-reduce | flops 8192 | bytes 32768 | tf_op jit(solution)/shard_map/psum | solution.py:58
  33.3 13.2 %all_gather.55 = bf16[32,1024]{1,0:T(8,128)(2,1)S(1)} all-gather(bf16[32,256]{1,0:T(8,128)(2,1)S(1)} %fusion.110), channel_id=1, replica_groups=mesh['grp'=2,'row'=4,'col'=2,'vec'=2] {'row'}, dimensions={1}, use_global_device_ids=true | all-gather | bytes 81920 | tf_op jit(solution)/shard_map/all_gather | solution.py:54
  46.5 0.6 gather_fusion.1
  47.6 7.2 %psum.135 = bf16[32,256]{1,0:T(8,128)(2,1)S(1)} all-reduce(bf16[32,256]{1,0:T(8,128)(2,1)S(1)} %bitcast.396), channel_id=1, replica_groups=mesh['grp'=2,'row'=4,'col'=2,'vec'=2] {'col'}, use_global_device_ids=true, to_apply=%region_2.4 | all-reduce | flops 8192 | bytes 32768 | tf_op jit(solution)/shard_map/psum | solution.py:58
  54.8 13.3 %all_gather.56 = bf16[32,1024]{1,0:T(8,128)(2,1)S(1)} all-gather(bf16[32,256]{1,0:T(8,128)(2,1)S(1)} %fusion.113), channel_id=1, replica_groups=mesh['grp'=2,'row'=4,'col'=2,'vec'=2] {'row'}, dimensions={1}, use_global_device_ids=true | all-gather | bytes 81920 | tf_op jit(solution)/shard_map/all_gather | solution.py:54
  68.1 0.6 gather_fusion.2
  69.2 8.1 %psum.136 = bf16[32,256]{1,0:T(8,128)(2,1)S(1)} all-reduce(bf16[32,256]{1,0:T(8,128)(2,1)S(1)} %bitcast.397), channel_id=1, replica_groups=mesh['grp'=2,'row'=4,'col'=2,'vec'=2] {'col'}, use_global_device_ids=true, to_apply=%region_3.5 | all-reduce | flops 8192 | bytes 32768 | tf_op jit(solution)/shard_map/psum | solution.py:58
  77.4 13.2 %all_gather.57 = bf16[32,1024]{1,0:T(8,128)(2,1)S(1)} all-gather(bf16[32,256]{1,0:T(8,128)(2,1)S(1)} %fusion.111), channel_id=1, replica_groups=mesh['grp'=2,'row'=4,'col'=2,'vec'=2] {'row'}, dimensions={1}, use_global_device_ids=true | all-gather | bytes 81920 | tf_op jit(solution)/shard_map/all_gather | solution.py:54
  90.6 0.6 gather_fusion.3
  91.7 7.2 %psum.137 = bf16[32,256]{1,0:T(8,128)(2,1)S(1)} all-reduce(bf16[32,256]{1,0:T(8,128)(2,1)S(1)} %bitcast.398), channel_id=1, replica_groups=mesh['grp'=2,'row'=4,'col'=2,'vec'=2] {'col'}, use_global_device_ids=true, to_apply=%region_4.6 | all-reduce | flops 8192 | bytes 32768 | tf_op jit(solution)/shard_map/psum | solution.py:58
  98.9 13.2 %all_gather.58 = bf16[32,1024]{1,0:T(8,128)(2,1)S(1)} all-gather(bf16[32,256]{1,0:T(8,128)(2,1)S(1)} %fusion.137), channel_id=1, replica_groups=mesh['grp'=2,'row'=4,'col'=2,'vec'=2] {'row'}, dimensions={1}, use_global_device_ids=true | all-gather | bytes 81920 | tf_op jit(solution)/shard_map/all_gather | solution.py:54
  112.1 0.6 gather_fusion.4
  113.3 8.1 %psum.138 = bf16[32,256]{1,0:T(8,128)(2,1)S(1)} all-reduce(bf16[32,256]{1,0:T(8,128)(2,1)S(1)} %bitcast.399), channel_id=1, replica_groups=mesh['grp'=2,'row'=4,'col'=2,'vec'=2] {'col'}, use_global_device_ids=true, to_apply=%region_5.7 | all-reduce | flops 8192 | bytes 32768 | tf_op jit(solution)/shard_map/psum | solution.py:58
  121.5 13.1 %all_gather.59 = bf16[32,1024]{1,0:T(8,128)(2,1)S(1)} all-gather(bf16[32,256]{1,0:T(8,128)(2,1)S(1)} %fusion.116), channel_id=1, replica_groups=mesh['grp'=2,'row'=4,'col'=2,'vec'=2] {'row'}, dimensions={1}, use_global_device_ids=true | all-gather | bytes 81920 | tf_op jit(solution)/shard_map/all_gather | solution.py:54
  134.6 0.6 gather_fusion.5
  135.8 7.3 %psum.139 = bf16[32,256]{1,0:T(8,128)(2,1)S(1)} all-reduce(bf16[32,256]{1,0:T(8,128)(2,1)S(1)} %bitcast.400), channel_id=1, replica_groups=mesh['grp'=2,'row'=4,'col'=2,'vec'=2] {'col'}, use_global_device_ids=true, to_apply=%region_6.8 | all-reduce | flops 8192 | bytes 32768 | tf_op jit(solution)/shard_map/psum | solution.py:58
  143.1 13.2 %all_gather.60 = bf16[32,1024]{1,0:T(8,128)(2,1)S(1)} all-gather(bf16[32,256]{1,0:T(8,128)(2,1)S(1)} %fusion.114), channel_id=1, replica_groups=mesh['grp'=2,'row'=4,'col'=2,'vec'=2] {'row'}, dimensions={1}, use_global_device_ids=true | all-gather | bytes 81920 | tf_op jit(solution)/shard_map/all_gather | solution.py:54
  156.3 0.6 gather_fusion.6
  157.4 8.0 %psum.140 = bf16[32,256]{1,0:T(8,128)(2,1)S(1)} all-reduce(bf16[32,256]{1,0:T(8,128)(2,1)S(1)} %bitcast.401), channel_id=1, replica_groups=mesh['grp'=2,'row'=4,'col'=2,'vec'=2] {'col'}, use_global_device_ids=true, to_apply=%region_7.9 | all-reduce | flops 8192 | bytes 32768 | tf_op jit(solution)/shard_map/psum | solution.py:58
  165.5 13.1 %all_gather.61 = bf16[32,1024]{1,0:T(8,128)(2,1)S(1)} all-gather(bf16[32,256]{1,0:T(8,128)(2,1)S(1)} %subtract_convert_fusion.3), channel_id=1, replica_groups=mesh['grp'=2,'row'=4,'col'=2,'vec'=2] {'row'}, dimensions={1}, use_global_device_ids=true | all-gather | bytes 81920 | tf_op jit(solution)/shard_map/all_gather | solution.py:54
  178.6 0.6 gather_fusion.7
  179.8 7.3 %psum.141 = bf16[32,256]{1,0:T(8,128)(2,1)S(1)} all-reduce(bf16[32,256]{1,0:T(8,128)(2,1)S(1)} %bitcast.402), channel_id=1, replica_groups=mesh['grp'=2,'row'=4,'col'=2,'vec'=2] {'col'}, use_global_device_ids=true, to_apply=%region_8.10 | all-reduce | flops 8192 | bytes 32768 | tf_op jit(solution)/shard_map/psum | solution.py:58
  187.1 1.8 all_gather.62
  189.1 18.8 %psum.142 = f32[64,64]{0,1:T(8,128)S(1)} all-reduce(f32[64,64]{0,1:T(8,128)S(1)} %fusion.138), channel_id=1, replica_groups=mesh['grp'=2,'row'=4,'col'=2,'vec'=2] {'row'}, use_global_device_ids=true, to_apply=%region_9.11 | all-reduce | flops 4096 | bytes 32768 | tf_op jit(solution)/shard_map/psum | solution.py:29
  208.1 5.8 %cholesky.44 = f32[64,64]{1,0:T(8,128)S(1)} custom-call(f32[64,64]{1,0:T(8,128)S(1)} %fusion.106), custom_call_target="Cholesky" | custom-call | tf_op jit(solution)/shard_map/jit(cholesky)/cholesky | solution.py:30
  213.9 0.6 compare_reduce_fusion.1
  214.6 0.7 fusion.101
  215.2 4.9 %custom-call.6 = f32[1,64,64]{1,2,0:T(8,128)S(1)} custom-call(f32[1,64,64]{2,1,0:T(8,128)S(1)} %fusion.101), custom_call_target="InvertDiagBlocksLowerTriangular" | custom-call | tf_op jit(solution)/shard_map/jit(_solve_triangular)/triangular_solve | solution.py:31
  220.4 13.1 %all_gather.63 = bf16[32,1024]{1,0:T(8,128)(2,1)S(1)} all-gather(bf16[32,256]{1,0:T(8,128)(2,1)S(1)} %dynamic-slice_convert_fusion), channel_id=1, replica_groups=mesh['grp'=2,'row'=4,'col'=2,'vec'=2] {'row'}, dimensions={1}, use_global_device_ids=true | all-gather | bytes 81920 | tf_op jit(solution)/shard_map/all_gather | solution.py:54
  233.6 0.6 gather_fusion.8
  234.7 8.0 %psum.143 = bf16[32,256]{1,0:T(8,128)(2,1)S(1)} all-reduce(bf16[32,256]{1,0:T(8,128)(2,1)S(1)} %bitcast.403), channel_id=1, replica_groups=mesh['grp'=2,'row'=4,'col'=2,'vec'=2] {'col'}, use_global_device_ids=true, to_apply=%region_12.16 | all-reduce | flops 8192 | bytes 32768 | tf_op jit(solution)/shard_map/psum | solution.py:58
  242.8 13.2 %all_gather.64 = bf16[32,1024]{1,0:T(8,128)(2,1)S(1)} all-gather(bf16[32,256]{1,0:T(8,128)(2,1)S(1)} %fusion.109), channel_id=1, replica_groups=mesh['grp'=2,'row'=4,'col'=2,'vec'=2] {'row'}, dimensions={1}, use_global_device_ids=true | all-gather | bytes 81920 | tf_op jit(solution)/shard_map/all_gather | solution.py:54
  256.0 0.6 gather_fusion.9
  257.1 7.3 %psum.144 = bf16[32,256]{1,0:T(8,128)(2,1)S(1)} all-reduce(bf16[32,256]{1,0:T(8,128)(2,1)S(1)} %bitcast.404), channel_id=1, replica_groups=mesh['grp'=2,'row'=4,'col'=2,'vec'=2] {'col'}, use_global_device_ids=true, to_apply=%region_13.17 | all-reduce | flops 8192 | bytes 32768 | tf_op jit(solution)/shard_map/psum | solution.py:58
  264.4 13.1 %all_gather.65 = bf16[32,1024]{1,0:T(8,128)(2,1)S(1)} all-gather(bf16[32,256]{1,0:T(8,128)(2,1)S(1)} %fusion.136), channel_id=1, replica_groups=mesh['grp'=2,'row'=4,'col'=2,'vec'=2] {'row'}, dimensions={1}, use_global_device_ids=true | all-gather | bytes 81920 | tf_op jit(solution)/shard_map/all_gather | solution.py:54
  277.6 0.6 gather_fusion.10
  278.8 8.0 %psum.145 = bf16[32,256]{1,0:T(8,128)(2,1)S(1)} all-reduce(bf16[32,256]{1,0:T(8,128)(2,1)S(1)} %bitcast.405), channel_id=1, replica_groups=mesh['grp'=2,'row'=4,'col'=2,'vec'=2] {'col'}, use_global_device_ids=true, to_apply=%region_14.18 | all-reduce | flops 8192 | bytes 32768 | tf_op jit(solution)/shard_map/psum | solution.py:58
  286.8 13.1 %all_gather.66 = bf16[32,1024]{1,0:T(8,128)(2,1)S(1)} all-gather(bf16[32,256]{1,0:T(8,128)(2,1)S(1)} %fusion.112), channel_id=1, replica_groups=mesh['grp'=2,'row'=4,'col'=2,'vec'=2] {'row'}, dimensions={1}, use_global_device_ids=true | all-gather | bytes 81920 | tf_op jit(solution)/shard_map/all_gather | solution.py:54
  300.0 0.6 gather_fusion.11
  301.1 7.3 %psum.146 = bf16[32,256]{1,0:T(8,128)(2,1)S(1)} all-reduce(bf16[32,256]{1,0:T(8,128)(2,1)S(1)} %bitcast.406), channel_id=1, replica_groups=mesh['grp'=2,'row'=4,'col'=2,'vec'=2] {'col'}, use_global_device_ids=true, to_apply=%region_15.19 | all-reduce | flops 8192 | bytes 32768 | tf_op jit(solution)/shard_map/psum | solution.py:58
  308.5 13.2 %all_gather.67 = bf16[32,1024]{1,0:T(8,128)(2,1)S(1)} all-gather(bf16[32,256]{1,0:T(8,128)(2,1)S(1)} %fusion.115), channel_id=1, replica_groups=mesh['grp'=2,'row'=4,'col'=2,'vec'=2] {'row'}, dimensions={1}, use_global_device_ids=true | all-gather | bytes 81920 | tf_op jit(solution)/shard_map/all_gather | solution.py:54
  321.7 0.6 gather_fusion.12
  322.8 8.0 %psum.147 = bf16[32,256]{1,0:T(8,128)(2,1)S(1)} all-reduce(bf16[32,256]{1,0:T(8,128)(2,1)S(1)} %bitcast.407), channel_id=1, replica_groups=mesh['grp'=2,'row'=4,'col'=2,'vec'=2] {'col'}, use_global_device_ids=true, to_apply=%region_16.20 | all-reduce | flops 8192 | bytes 32768 | tf_op jit(solution)/shard_map/psum | solution.py:58
  330.8 13.3 %all_gather.68 = bf16[32,1024]{1,0:T(8,128)(2,1)S(1)} all-gather(bf16[32,256]{1,0:T(8,128)(2,1)S(1)} %fusion.117), channel_id=1, replica_groups=mesh['grp'=2,'row'=4,'col'=2,'vec'=2] {'row'}, dimensions={1}, use_global_device_ids=true | all-gather | bytes 81920 | tf_op jit(solution)/shard_map/all_gather | solution.py:54
  344.2 0.6 gather_fusion.13
  345.3 7.4 %psum.148 = bf16[32,256]{1,0:T(8,128)(2,1)S(1)} all-reduce(bf16[32,256]{1,0:T(8,128)(2,1)S(1)} %bitcast.408), channel_id=1, replica_groups=mesh['grp'=2,'row'=4,'col'=2,'vec'=2] {'col'}, use_global_device_ids=true, to_apply=%region_17.21 | all-reduce | flops 8192 | bytes 32768 | tf_op jit(solution)/shard_map/psum | solution.py:58
  352.7 13.1 %all_gather.69 = bf16[32,1024]{1,0:T(8,128)(2,1)S(1)} all-gather(bf16[32,256]{1,0:T(8,128)(2,1)S(1)} %fusion.118), channel_id=1, replica_groups=mesh['grp'=2,'row'=4,'col'=2,'vec'=2] {'row'}, dimensions={1}, use_global_device_ids=true | all-gather | bytes 81920 | tf_op jit(solution)/shard_map/all_gather | solution.py:54
  367.0 8.0 %psum.149 = bf16[32,256]{1,0:T(8,128)(2,1)S(1)} all-reduce(bf16[32,256]{1,0:T(8,128)(2,1)S(1)} %bitcast.409), channel_id=1, replica_groups=mesh['grp'=2,'row'=4,'col'=2,'vec'=2] {'col'}, use_global_device_ids=true, to_apply=%region_18.22 | all-reduce | flops 8192 | bytes 32768 | tf_op jit(solution)/shard_map/psum | solution.py:58
  375.0 13.1 %all_gather.70 = bf16[32,1024]{1,0:T(8,128)(2,1)S(1)} all-gather(bf16[32,256]{1,0:T(8,128)(2,1)S(1)} %subtract_convert_fusion.1), channel_id=1, replica_groups=mesh['grp'=2,'row'=4,'col'=2,'vec'=2] {'row'}, dimensions={1}, use_global_device_ids=true | all-gather | bytes 81920 | tf_op jit(solution)/shard_map/all_gather | solution.py:54
  389.3 7.4 %psum.150 = bf16[32,256]{1,0:T(8,128)(2,1)S(1)} all-reduce(bf16[32,256]{1,0:T(8,128)(2,1)S(1)} %bitcast.410), channel_id=1, replica_groups=mesh['grp'=2,'row'=4,'col'=2,'vec'=2] {'col'}, use_global_device_ids=true, to_apply=%region_19.23 | all-reduce | flops 8192 | bytes 32768 | tf_op jit(solution)/shard_map/psum | solution.py:58
  396.8 1.8 all_gather.71
  398.7 15.9 %psum.151 = f32[64,64]{0,1:T(8,128)S(1)} all-reduce(f32[64,64]{0,1:T(8,128)S(1)} %fusion.139), channel_id=1, replica_groups=mesh['grp'=2,'row'=4,'col'=2,'vec'=2] {'row'}, use_global_device_ids=true, to_apply=%region_20.24 | all-reduce | flops 4096 | bytes 32768 | tf_op jit(solution)/shard_map/psum | solution.py:29
  414.7 5.8 %cholesky.55 = f32[64,64]{1,0:T(8,128)S(1)} custom-call(f32[64,64]{1,0:T(8,128)S(1)} %fusion.104), custom_call_target="Cholesky" | custom-call | tf_op jit(solution)/shard_map/jit(cholesky)/cholesky | solution.py:30
  420.6 0.6 compare_reduce_fusion
  421.3 0.7 fusion.102
  421.9 4.9 %custom-call.7 = f32[1,64,64]{1,2,0:T(8,128)S(1)} custom-call(f32[1,64,64]{2,1,0:T(8,128)S(1)} %fusion.102), custom_call_target="InvertDiagBlocksLowerTriangular" | custom-call | tf_op jit(solution)/shard_map/jit(_solve_triangular)/triangular_solve | solution.py:31
  427.1 0.6 constant_dynamic-slice_fusion
  (91 shorter events, 11.5 us)
Async XLA Ops:
  0.0 24.5 %copy-start = (bf16[2,16,128,128]{3,2,1,0:T(8,128)(2,1)S(1)}, bf16[2,16,128,128]{3,2,1,0:T(8,128)(2,1)}, u32[]{:S(2)}) copy-start(bf16[2,16,128,128]{3,2,1,0:T(8,128)(2,1)} %param.10) | copy-start | bytes 3145732
  0.0 9.9 %copy-start.1 = (f32[32,256]{1,0:T(8,128)S(1)}, f32[32,256]{1,0:T(8,128)}, u32[]{:S(2)}) copy-start(f32[32,256]{1,0:T(8,128)} %param.9) | copy-start | bytes 98308
  0.0 9.7 %copy-start.2 = (s32[2,32]{1,0:T(2,128)S(1)}, s32[2,32]{1,0:T(2,128)}, u32[]{:S(2)}) copy-start(s32[2,32]{1,0:T(2,128)} %param.11) | copy-start | bytes 772
where the time goes:
time: 429 us; the launch traced here: 428 us
  blocking collectives  379 us (88%)
  other arithmetic  28.4 us (7%)
  local copies, waits for them, and re-layouts  11 us (3%)
  matrix products  9.04 us (2%)
    all_gather x16, blocking collectives, apply_slots(): lax.all_gather(current.astype(jnp.bfloat16), 'row', axis=1, tiled=True)  212 us
    psum x16, blocking collectives, apply_slots(): total = lax.psum(product.astype(jnp.bfloat16), 'col').astype(jnp.float32)  123 us
    psum x2, blocking collectives, orthonormal(): gram = lax.psum(part_gram, 'row') / total_rows  34.8 us
    another operation x6, other arithmetic, orthonormal(): lower = jnp.linalg.cholesky(gram)  13 us
    another operation x4, other arithmetic, orthonormal(): solved = jax.scipy.linalg.solve_triangular(lower, both, lower=True)  11.1 us
    gather x16, local copies, waits for them, and re-layouts, apply_slots(): picked = jnp.take(blocks, local_pattern, axis=1)  9.63 us

commit v1 on v0

--- a/solution.py
+++ b/solution.py
@@ -51,7 +51,16 @@
     scaling = row_scaling(square_sums, counts, block)
 
     def apply_slots(current):
-        whole = lax.all_gather(current.astype(jnp.bfloat16), "row", axis=1, tiled=True)
+        x = current.astype(jnp.bfloat16)
+        ways, here, step_2 = (lax.axis_size("row"), lax.axis_index("row"), x.shape[1])
+        line, have = (x, 1)
+        while have < ways:
+            line = jnp.concatenate(
+                [line, lax.ppermute(line, "row", [(d, (d - have) % ways) for d in range(ways)])],
+                axis=1,
+            )
+            have = 2 * have
+        whole = jnp.roll(line, here * step_2, axis=1)
         blocks = whole.reshape(vec_cols, -1, block)
         picked = jnp.take(blocks, local_pattern, axis=1)
         product = jnp.einsum("cbkn,bkmn->cbm", picked, masked, preferred_element_type=jnp.float32)

time: 429 us -> 383 us (0.89)
  blocking collectives: 379 us -> 171 us
  waiting for transfers between devices: 0 us -> 92.3 us
  starting transfers between devices: 0 us -> 66.4 us
    all_gather x16 -> x0, blocking collectives: 212 us -> none  [apply_slots(): lax.all_gather(current.astype(jnp.bfloat16), 'row', axis=1, tiled=True)]
    ppermute x0 -> x32, waiting for transfers between devices: none -> 92.3 us  [apply_slots(): lax.ppermute(line, 'row', [(d, (d - have) % ways) for d in range(ways)])]
    ppermute x0 -> x32, starting transfers between devices: none -> 66.4 us  [apply_slots(): lax.ppermute(line, 'row', [(d, (d - have) % ways) for d in range(ways)])]
    psum x2, blocking collectives: 34.8 us -> 39.6 us  [orthonormal(): gram = lax.psum(part_gram, 'row') / total_rows]
  transfers between devices with their start and end apart: 0 -> 32, of which waited for: 0 -> 31; matrix products, arithmetic and copies ran while one was open for 0% -> 1% of each run, Pallas kernels for 0% -> 0%
where the time goes in v1:
time: 383 us; the launch traced here: 382 us
  blocking collectives  171 us (45%)
  waiting for transfers between devices  92.3 us (24%)
  starting transfers between devices  66.4 us (17%)
  other arithmetic  31.8 us (8%)
  local copies, waits for them, and re-layouts  10.8 us (3%)
  matrix products  9.04 us (2%)
    psum x16, blocking collectives, apply_slots(): total = lax.psum(product.astype(jnp.bfloat16), 'col').astype(jnp.float32)  123 us
    ppermute x32, waiting for transfers between devices, apply_slots(): lax.ppermute(line, 'row', [(d, (d - have) % ways) for d in range(ways)])  92.3 us
    ppermute x32, starting transfers between devices, apply_slots(): lax.ppermute(line, 'row', [(d, (d - have) % ways) for d in range(ways)])  66.4 us
    psum x2, blocking collectives, orthonormal(): gram = lax.psum(part_gram, 'row') / total_rows  39.6 us
    another operation x6, other arithmetic, orthonormal(): lower = jnp.linalg.cholesky(gram)  13 us
    another operation x4, other arithmetic, orthonormal(): solved = jax.scipy.linalg.solve_triangular(lower, both, lower=True)  11.1 us
    gather x16, local copies, waits for them, and re-layouts, apply_slots(): picked = jnp.take(blocks, local_pattern, axis=1)  9.63 us
    dot_general x16, matrix products, apply_slots(): jnp.einsum('cbkn,bkmn->cbm', picked, masked, preferred_element_type=jnp.f...  8.26 us
  transfers between devices with their start and end apart: 32, of which 31 were waited for; matrix products, arithmetic and copies ran while one was open for 1% of the time, Pallas kernels for 0%

profile of v1, /device:TPU:0, one launch (start us, length us, event | category | flops | bytes accessed | tf_op | source)
XLA Modules:
  0.0 382.1 jit_solution(10160160881308234227)
XLA Ops:
  0.9 5.0 %collective-permute-start = (bf16[32,256]{1,0:T(8,128)(2,1)S(1)}, bf16[32,256]{1,0:T(8,128)(2,1)S(1)}, u32[]{:S(2)}, u32[]{:S(2)}) collective-permute-start(bf16[32,256]{1,0:T(8,128)(2,1)S(1)} %convert_element_type.183), channel_id=1, source_target_pairs={{0,12},{4,0},{8,4},{12,8},{1,13},{5,1},{9,5},{13,9},{2,14},{6,2},{... | collective-permute-start | bytes 49160 | tf_op jit(solution)/shard_map/ppermute | solution.py:59
  8.0 1.6 fusion
  9.6 4.9 %psum.134 = f32[2,128]{1,0:T(2,128)S(1)} all-reduce(f32[2,128]{1,0:T(2,128)S(1)} %fusion), channel_id=1, replica_groups=mesh['grp'=2,'row'=4,'col'=2,'vec'=2] {'col'}, use_global_device_ids=true, to_apply=%region_1.4 | all-reduce | flops 256 | bytes 2048 | tf_op jit(solution)/shard_map/psum | solution.py:50
  14.9 4.8 %collective-permute-done.1 = bf16[32,512]{1,0:T(8,128)(2,1)S(1)} collective-permute-done((bf16[32,512]{1,0:T(8,128)(2,1)S(1)}, bf16[32,512]{1,0:T(8,128)(2,1)S(1)}, u32[]{:S(2)}, u32[]{:S(2)}) %collective-permute-start.1) | collective-permute-done | bytes 32800 | tf_op jit(solution)/shard_map/ppermute | solution.py:59
  21.0 8.2 %psum.133 = bf16[32,256]{1,0:T(8,128)(2,1)S(1)} all-reduce(bf16[32,256]{1,0:T(8,128)(2,1)S(1)} %bitcast.395), channel_id=1, replica_groups=mesh['grp'=2,'row'=4,'col'=2,'vec'=2] {'col'}, use_global_device_ids=true, to_apply=%region_0.3 | all-reduce | flops 8192 | bytes 32768 | tf_op jit(solution)/shard_map/psum | solution.py:67
  29.7 3.3 collective-permute-done.2
  33.0 4.8 %collective-permute-done.3 = bf16[32,512]{1,0:T(8,128)(2,1)S(1)} collective-permute-done((bf16[32,512]{1,0:T(8,128)(2,1)S(1)}, bf16[32,512]{1,0:T(8,128)(2,1)S(1)}, u32[]{:S(2)}, u32[]{:S(2)}) %collective-permute-start.3) | collective-permute-done | bytes 32800 | tf_op jit(solution)/shard_map/ppermute | solution.py:59
  39.1 7.2 %psum.135 = bf16[32,256]{1,0:T(8,128)(2,1)S(1)} all-reduce(bf16[32,256]{1,0:T(8,128)(2,1)S(1)} %bitcast.396), channel_id=1, replica_groups=mesh['grp'=2,'row'=4,'col'=2,'vec'=2] {'col'}, use_global_device_ids=true, to_apply=%region_2.5 | all-reduce | flops 8192 | bytes 32768 | tf_op jit(solution)/shard_map/psum | solution.py:67
  46.3 2.3 collective-permute-start.4
  48.6 1.5 collective-permute-done.4
  50.9 4.0 %collective-permute-done.5 = bf16[32,512]{1,0:T(8,128)(2,1)S(1)} collective-permute-done((bf16[32,512]{1,0:T(8,128)(2,1)S(1)}, bf16[32,512]{1,0:T(8,128)(2,1)S(1)}, u32[]{:S(2)}, u32[]{:S(2)}) %collective-permute-start.5) | collective-permute-done | bytes 32800 | tf_op jit(solution)/shard_map/ppermute | solution.py:59
  56.3 8.3 %psum.136 = bf16[32,256]{1,0:T(8,128)(2,1)S(1)} all-reduce(bf16[32,256]{1,0:T(8,128)(2,1)S(1)} %bitcast.397), channel_id=1, replica_groups=mesh['grp'=2,'row'=4,'col'=2,'vec'=2] {'col'}, use_global_device_ids=true, to_apply=%region_3.6 | all-reduce | flops 8192 | bytes 32768 | tf_op jit(solution)/shard_map/psum | solution.py:67
  64.6 3.9 %collective-permute-start.6 = (bf16[32,256]{1,0:T(8,128)(2,1)S(1)}, bf16[32,256]{1,0:T(8,128)(2,1)S(1)}, u32[]{:S(2)}, u32[]{:S(2)}) collective-permute-start(bf16[32,256]{1,0:T(8,128)(2,1)S(1)} %fusion.207), channel_id=1, source_target_pairs={{0,12},{4,0},{8,4},{12,8},{1,13},{5,1},{9,5},{13,9},{2,14},{6,2},{... | collective-permute-start | bytes 49160 | tf_op jit(solution)/shard_map/ppermute | solution.py:59
  68.5 1.4 collective-permute-done.6
  70.8 4.1 %collective-permute-done.7 = bf16[32,512]{1,0:T(8,128)(2,1)S(1)} collective-permute-done((bf16[32,512]{1,0:T(8,128)(2,1)S(1)}, bf16[32,512]{1,0:T(8,128)(2,1)S(1)}, u32[]{:S(2)}, u32[]{:S(2)}) %collective-permute-start.7) | collective-permute-done | bytes 32800 | tf_op jit(solution)/shard_map/ppermute | solution.py:59
  76.3 7.0 %psum.137 = bf16[32,256]{1,0:T(8,128)(2,1)S(1)} all-reduce(bf16[32,256]{1,0:T(8,128)(2,1)S(1)} %bitcast.398), channel_id=1, replica_groups=mesh['grp'=2,'row'=4,'col'=2,'vec'=2] {'col'}, use_global_device_ids=true, to_apply=%region_4.7 | all-reduce | flops 8192 | bytes 32768 | tf_op jit(solution)/shard_map/psum | solution.py:67
  83.3 4.2 %collective-permute-start.8 = (bf16[32,256]{1,0:T(8,128)(2,1)S(1)}, bf16[32,256]{1,0:T(8,128)(2,1)S(1)}, u32[]{:S(2)}, u32[]{:S(2)}) collective-permute-start(bf16[32,256]{1,0:T(8,128)(2,1)S(1)} %fusion.233), channel_id=1, source_target_pairs={{0,12},{4,0},{8,4},{12,8},{1,13},{5,1},{9,5},{13,9},{2,14},{6,2},{... | collective-permute-start | bytes 49160 | tf_op jit(solution)/shard_map/ppermute | solution.py:59
  87.6 1.4 collective-permute-done.8
  89.9 4.0 %collective-permute-done.9 = bf16[32,512]{1,0:T(8,128)(2,1)S(1)} collective-permute-done((bf16[32,512]{1,0:T(8,128)(2,1)S(1)}, bf16[32,512]{1,0:T(8,128)(2,1)S(1)}, u32[]{:S(2)}, u32[]{:S(2)}) %collective-permute-start.9) | collective-permute-done | bytes 32800 | tf_op jit(solution)/shard_map/ppermute | solution.py:59
  95.1 8.3 %psum.138 = bf16[32,256]{1,0:T(8,128)(2,1)S(1)} all-reduce(bf16[32,256]{1,0:T(8,128)(2,1)S(1)} %bitcast.399), channel_id=1, replica_groups=mesh['grp'=2,'row'=4,'col'=2,'vec'=2] {'col'}, use_global_device_ids=true, to_apply=%region_5.8 | all-reduce | flops 8192 | bytes 32768 | tf_op jit(solution)/shard_map/psum | solution.py:67
  103.5 4.1 %collective-permute-start.10 = (bf16[32,256]{1,0:T(8,128)(2,1)S(1)}, bf16[32,256]{1,0:T(8,128)(2,1)S(1)}, u32[]{:S(2)}, u32[]{:S(2)}) collective-permute-start(bf16[32,256]{1,0:T(8,128)(2,1)S(1)} %fusion.212), channel_id=1, source_target_pairs={{0,12},{4,0},{8,4},{12,8},{1,13},{5,1},{9,5},{13,9},{2,14},{6,2},{... | collective-permute-start | bytes 49160 | tf_op jit(solution)/shard_map/ppermute | solution.py:59
  109.9 4.0 %collective-permute-done.11 = bf16[32,512]{1,0:T(8,128)(2,1)S(1)} collective-permute-done((bf16[32,512]{1,0:T(8,128)(2,1)S(1)}, bf16[32,512]{1,0:T(8,128)(2,1)S(1)}, u32[]{:S(2)}, u32[]{:S(2)}) %collective-permute-start.11) | collective-permute-done | bytes 32800 | tf_op jit(solution)/shard_map/ppermute | solution.py:59
  115.2 7.1 %psum.139 = bf16[32,256]{1,0:T(8,128)(2,1)S(1)} all-reduce(bf16[32,256]{1,0:T(8,128)(2,1)S(1)} %bitcast.400), channel_id=1, replica_groups=mesh['grp'=2,'row'=4,'col'=2,'vec'=2] {'col'}, use_global_device_ids=true, to_apply=%region_6.9 | all-reduce | flops 8192 | bytes 32768 | tf_op jit(solution)/shard_map/psum | solution.py:67
  122.3 4.1 %collective-permute-start.12 = (bf16[32,256]{1,0:T(8,128)(2,1)S(1)}, bf16[32,256]{1,0:T(8,128)(2,1)S(1)}, u32[]{:S(2)}, u32[]{:S(2)}) collective-permute-start(bf16[32,256]{1,0:T(8,128)(2,1)S(1)} %fusion.210), channel_id=1, source_target_pairs={{0,12},{4,0},{8,4},{12,8},{1,13},{5,1},{9,5},{13,9},{2,14},{6,2},{... | collective-permute-start | bytes 49160 | tf_op jit(solution)/shard_map/ppermute | solution.py:59
  126.4 1.4 collective-permute-done.12
  128.7 4.0 %collective-permute-done.13 = bf16[32,512]{1,0:T(8,128)(2,1)S(1)} collective-permute-done((bf16[32,512]{1,0:T(8,128)(2,1)S(1)}, bf16[32,512]{1,0:T(8,128)(2,1)S(1)}, u32[]{:S(2)}, u32[]{:S(2)}) %collective-permute-start.13) | collective-permute-done | bytes 32800 | tf_op jit(solution)/shard_map/ppermute | solution.py:59
  134.0 8.3 %psum.140 = bf16[32,256]{1,0:T(8,128)(2,1)S(1)} all-reduce(bf16[32,256]{1,0:T(8,128)(2,1)S(1)} %bitcast.401), channel_id=1, replica_groups=mesh['grp'=2,'row'=4,'col'=2,'vec'=2] {'col'}, use_global_device_ids=true, to_apply=%region_7.10 | all-reduce | flops 8192 | bytes 32768 | tf_op jit(solution)/shard_map/psum | solution.py:67
  142.3 4.1 %collective-permute-start.14 = (bf16[32,256]{1,0:T(8,128)(2,1)S(1)}, bf16[32,256]{1,0:T(8,128)(2,1)S(1)}, u32[]{:S(2)}, u32[]{:S(2)}) collective-permute-start(bf16[32,256]{1,0:T(8,128)(2,1)S(1)} %subtract_convert_fusion.3), channel_id=1, source_target_pairs={{0,12},{4,0},{8,4},{12,8},{1,13},{5,1},{9,5},{13,9},{2,14},{6,2},{... | collective-permute-start | bytes 49160 | tf_op jit(solution)/shard_map/ppermute | solution.py:59
  146.5 1.4 collective-permute-done.14
  148.8 4.0 %collective-permute-done.15 = bf16[32,512]{1,0:T(8,128)(2,1)S(1)} collective-permute-done((bf16[32,512]{1,0:T(8,128)(2,1)S(1)}, bf16[32,512]{1,0:T(8,128)(2,1)S(1)}, u32[]{:S(2)}, u32[]{:S(2)}) %collective-permute-start.15) | collective-permute-done | bytes 32800 | tf_op jit(solution)/shard_map/ppermute | solution.py:59
  154.1 7.1 %psum.141 = bf16[32,256]{1,0:T(8,128)(2,1)S(1)} all-reduce(bf16[32,256]{1,0:T(8,128)(2,1)S(1)} %bitcast.402), channel_id=1, replica_groups=mesh['grp'=2,'row'=4,'col'=2,'vec'=2] {'col'}, use_global_device_ids=true, to_apply=%region_8.11 | all-reduce | flops 8192 | bytes 32768 | tf_op jit(solution)/shard_map/psum | solution.py:67
  161.1 1.8 all_gather.6
  163.1 19.8 %psum.142 = f32[64,64]{0,1:T(8,128)S(1)} all-reduce(f32[64,64]{0,1:T(8,128)S(1)} %fusion.234), channel_id=1, replica_groups=mesh['grp'=2,'row'=4,'col'=2,'vec'=2] {'row'}, use_global_device_ids=true, to_apply=%region_9.12 | all-reduce | flops 4096 | bytes 32768 | tf_op jit(solution)/shard_map/psum | solution.py:29
  183.0 5.8 %cholesky.44 = f32[64,64]{1,0:T(8,128)S(1)} custom-call(f32[64,64]{1,0:T(8,128)S(1)} %fusion.202), custom_call_target="Cholesky" | custom-call | tf_op jit(solution)/shard_map/jit(cholesky)/cholesky | solution.py:30
  190.2 4.9 %custom-call.6 = f32[1,64,64]{1,2,0:T(8,128)S(1)} custom-call(f32[1,64,64]{2,1,0:T(8,128)S(1)} %fusion.197), custom_call_target="InvertDiagBlocksLowerTriangular" | custom-call | tf_op jit(solution)/shard_map/jit(_solve_triangular)/triangular_solve | solution.py:31
  195.4 3.7 collective-permute-done.16
  199.8 4.2 %collective-permute-done.17 = bf16[32,512]{1,0:T(8,128)(2,1)S(1)} collective-permute-done((bf16[32,512]{1,0:T(8,128)(2,1)S(1)}, bf16[32,512]{1,0:T(8,128)(2,1)S(1)}, u32[]{:S(2)}, u32[]{:S(2)}) %collective-permute-start.17) | collective-permute-done | bytes 32800 | tf_op jit(solution)/shard_map/ppermute | solution.py:59
  205.3 8.3 %psum.143 = bf16[32,256]{1,0:T(8,128)(2,1)S(1)} all-reduce(bf16[32,256]{1,0:T(8,128)(2,1)S(1)} %bitcast.403), channel_id=1, replica_groups=mesh['grp'=2,'row'=4,'col'=2,'vec'=2] {'col'}, use_global_device_ids=true, to_apply=%region_12.17 | all-reduce | flops 8192 | bytes 32768 | tf_op jit(solution)/shard_map/psum | solution.py:67
  213.6 1.9 collective-permute-start.18
  215.5 1.9 collective-permute-done.18
  218.0 4.2 %collective-permute-done.19 = bf16[32,512]{1,0:T(8,128)(2,1)S(1)} collective-permute-done((bf16[32,512]{1,0:T(8,128)(2,1)S(1)}, bf16[32,512]{1,0:T(8,128)(2,1)S(1)}, u32[]{:S(2)}, u32[]{:S(2)}) %collective-permute-start.19) | collective-permute-done | bytes 32800 | tf_op jit(solution)/shard_map/ppermute | solution.py:59
  223.6 7.1 %psum.144 = bf16[32,256]{1,0:T(8,128)(2,1)S(1)} all-reduce(bf16[32,256]{1,0:T(8,128)(2,1)S(1)} %bitcast.404), channel_id=1, replica_groups=mesh['grp'=2,'row'=4,'col'=2,'vec'=2] {'col'}, use_global_device_ids=true, to_apply=%region_13.18 | all-reduce | flops 8192 | bytes 32768 | tf_op jit(solution)/shard_map/psum | solution.py:67
  230.6 3.7 collective-permute-start.20
  236.6 4.0 %collective-permute-done.21 = bf16[32,512]{1,0:T(8,128)(2,1)S(1)} collective-permute-done((bf16[32,512]{1,0:T(8,128)(2,1)S(1)}, bf16[32,512]{1,0:T(8,128)(2,1)S(1)}, u32[]{:S(2)}, u32[]{:S(2)}) %collective-permute-start.21) | collective-permute-done | bytes 32800 | tf_op jit(solution)/shard_map/ppermute | solution.py:59
  241.9 8.3 %psum.145 = bf16[32,256]{1,0:T(8,128)(2,1)S(1)} all-reduce(bf16[32,256]{1,0:T(8,128)(2,1)S(1)} %bitcast.405), channel_id=1, replica_groups=mesh['grp'=2,'row'=4,'col'=2,'vec'=2] {'col'}, use_global_device_ids=true, to_apply=%region_14.19 | all-reduce | flops 8192 | bytes 32768 | tf_op jit(solution)/shard_map/psum | solution.py:67
  250.2 4.1 %collective-permute-start.22 = (bf16[32,256]{1,0:T(8,128)(2,1)S(1)}, bf16[32,256]{1,0:T(8,128)(2,1)S(1)}, u32[]{:S(2)}, u32[]{:S(2)}) collective-permute-start(bf16[32,256]{1,0:T(8,128)(2,1)S(1)} %fusion.208), channel_id=1, source_target_pairs={{0,12},{4,0},{8,4},{12,8},{1,13},{5,1},{9,5},{13,9},{2,14},{6,2},{... | collective-permute-start | bytes 49160 | tf_op jit(solution)/shard_map/ppermute | solution.py:59
  256.6 4.0 %collective-permute-done.23 = bf16[32,512]{1,0:T(8,128)(2,1)S(1)} collective-permute-done((bf16[32,512]{1,0:T(8,128)(2,1)S(1)}, bf16[32,512]{1,0:T(8,128)(2,1)S(1)}, u32[]{:S(2)}, u32[]{:S(2)}) %collective-permute-start.23) | collective-permute-done | bytes 32800 | tf_op jit(solution)/shard_map/ppermute | solution.py:59
  261.9 7.2 %psum.146 = bf16[32,256]{1,0:T(8,128)(2,1)S(1)} all-reduce(bf16[32,256]{1,0:T(8,128)(2,1)S(1)} %bitcast.406), channel_id=1, replica_groups=mesh['grp'=2,'row'=4,'col'=2,'vec'=2] {'col'}, use_global_device_ids=true, to_apply=%region_15.20 | all-reduce | flops 8192 | bytes 32768 | tf_op jit(solution)/shard_map/psum | solution.py:67
  269.2 4.3 %collective-permute-start.24 = (bf16[32,256]{1,0:T(8,128)(2,1)S(1)}, bf16[32,256]{1,0:T(8,128)(2,1)S(1)}, u32[]{:S(2)}, u32[]{:S(2)}) collective-permute-start(bf16[32,256]{1,0:T(8,128)(2,1)S(1)} %fusion.211), channel_id=1, source_target_pairs={{0,12},{4,0},{8,4},{12,8},{1,13},{5,1},{9,5},{13,9},{2,14},{6,2},{... | collective-permute-start | bytes 49160 | tf_op jit(solution)/shard_map/ppermute | solution.py:59
  275.8 4.0 %collective-permute-done.25 = bf16[32,512]{1,0:T(8,128)(2,1)S(1)} collective-permute-done((bf16[32,512]{1,0:T(8,128)(2,1)S(1)}, bf16[32,512]{1,0:T(8,128)(2,1)S(1)}, u32[]{:S(2)}, u32[]{:S(2)}) %collective-permute-start.25) | collective-permute-done | bytes 32800 | tf_op jit(solution)/shard_map/ppermute | solution.py:59
  281.1 8.0 %psum.147 = bf16[32,256]{1,0:T(8,128)(2,1)S(1)} all-reduce(bf16[32,256]{1,0:T(8,128)(2,1)S(1)} %bitcast.407), channel_id=1, replica_groups=mesh['grp'=2,'row'=4,'col'=2,'vec'=2] {'col'}, use_global_device_ids=true, to_apply=%region_16.21 | all-reduce | flops 8192 | bytes 32768 | tf_op jit(solution)/shard_map/psum | solution.py:67
  289.1 4.1 %collective-permute-start.26 = (bf16[32,256]{1,0:T(8,128)(2,1)S(1)}, bf16[32,256]{1,0:T(8,128)(2,1)S(1)}, u32[]{:S(2)}, u32[]{:S(2)}) collective-permute-start(bf16[32,256]{1,0:T(8,128)(2,1)S(1)} %fusion.213), channel_id=1, source_target_pairs={{0,12},{4,0},{8,4},{12,8},{1,13},{5,1},{9,5},{13,9},{2,14},{6,2},{... | collective-permute-start | bytes 49160 | tf_op jit(solution)/shard_map/ppermute | solution.py:59
  295.5 4.1 %collective-permute-done.27 = bf16[32,512]{1,0:T(8,128)(2,1)S(1)} collective-permute-done((bf16[32,512]{1,0:T(8,128)(2,1)S(1)}, bf16[32,512]{1,0:T(8,128)(2,1)S(1)}, u32[]{:S(2)}, u32[]{:S(2)}) %collective-permute-start.27) | collective-permute-done | bytes 32800 | tf_op jit(solution)/shard_map/ppermute | solution.py:59
  300.9 7.3 %psum.148 = bf16[32,256]{1,0:T(8,128)(2,1)S(1)} all-reduce(bf16[32,256]{1,0:T(8,128)(2,1)S(1)} %bitcast.408), channel_id=1, replica_groups=mesh['grp'=2,'row'=4,'col'=2,'vec'=2] {'col'}, use_global_device_ids=true, to_apply=%region_17.22 | all-reduce | flops 8192 | bytes 32768 | tf_op jit(solution)/shard_map/psum | solution.py:67
  308.3 4.3 %collective-permute-start.28 = (bf16[32,256]{1,0:T(8,128)(2,1)S(1)}, bf16[32,256]{1,0:T(8,128)(2,1)S(1)}, u32[]{:S(2)}, u32[]{:S(2)}) collective-permute-start(bf16[32,256]{1,0:T(8,128)(2,1)S(1)} %fusion.214), channel_id=1, source_target_pairs={{0,12},{4,0},{8,4},{12,8},{1,13},{5,1},{9,5},{13,9},{2,14},{6,2},{... | collective-permute-start | bytes 49160 | tf_op jit(solution)/shard_map/ppermute | solution.py:59
  314.8 4.0 %collective-permute-done.29 = bf16[32,512]{1,0:T(8,128)(2,1)S(1)} collective-permute-done((bf16[32,512]{1,0:T(8,128)(2,1)S(1)}, bf16[32,512]{1,0:T(8,128)(2,1)S(1)}, u32[]{:S(2)}, u32[]{:S(2)}) %collective-permute-start.29) | collective-permute-done | bytes 32800 | tf_op jit(solution)/shard_map/ppermute | solution.py:59
  320.1 7.8 %psum.149 = bf16[32,256]{1,0:T(8,128)(2,1)S(1)} all-reduce(bf16[32,256]{1,0:T(8,128)(2,1)S(1)} %bitcast.409), channel_id=1, replica_groups=mesh['grp'=2,'row'=4,'col'=2,'vec'=2] {'col'}, use_global_device_ids=true, to_apply=%region_18.23 | all-reduce | flops 8192 | bytes 32768 | tf_op jit(solution)/shard_map/psum | solution.py:67
  327.9 4.1 %collective-permute-start.30 = (bf16[32,256]{1,0:T(8,128)(2,1)S(1)}, bf16[32,256]{1,0:T(8,128)(2,1)S(1)}, u32[]{:S(2)}, u32[]{:S(2)}) collective-permute-start(bf16[32,256]{1,0:T(8,128)(2,1)S(1)} %subtract_convert_fusion.1), channel_id=1, source_target_pairs={{0,12},{4,0},{8,4},{12,8},{1,13},{5,1},{9,5},{13,9},{2,14},{6,2},{... | collective-permute-start | bytes 49160 | tf_op jit(solution)/shard_map/ppermute | solution.py:59
  334.4 4.0 %collective-permute-done.31 = bf16[32,512]{1,0:T(8,128)(2,1)S(1)} collective-permute-done((bf16[32,512]{1,0:T(8,128)(2,1)S(1)}, bf16[32,512]{1,0:T(8,128)(2,1)S(1)}, u32[]{:S(2)}, u32[]{:S(2)}) %collective-permute-start.31) | collective-permute-done | bytes 32800 | tf_op jit(solution)/shard_map/ppermute | solution.py:59
  339.7 7.6 %psum.150 = bf16[32,256]{1,0:T(8,128)(2,1)S(1)} all-reduce(bf16[32,256]{1,0:T(8,128)(2,1)S(1)} %bitcast.410), channel_id=1, replica_groups=mesh['grp'=2,'row'=4,'col'=2,'vec'=2] {'col'}, use_global_device_ids=true, to_apply=%region_19.24 | all-reduce | flops 8192 | bytes 32768 | tf_op jit(solution)/shard_map/psum | solution.py:67
  347.3 1.8 all_gather.7
  349.2 19.8 %psum.151 = f32[64,64]{0,1:T(8,128)S(1)} all-reduce(f32[64,64]{0,1:T(8,128)S(1)} %fusion.235), channel_id=1, replica_groups=mesh['grp'=2,'row'=4,'col'=2,'vec'=2] {'row'}, use_global_device_ids=true, to_apply=%region_20.25 | all-reduce | flops 4096 | bytes 32768 | tf_op jit(solution)/shard_map/psum | solution.py:29
  369.1 5.8 %cholesky.55 = f32[64,64]{1,0:T(8,128)S(1)} custom-call(f32[64,64]{1,0:T(8,128)S(1)} %fusion.200), custom_call_target="Cholesky" | custom-call | tf_op jit(solution)/shard_map/jit(cholesky)/cholesky | solution.py:30
  376.3 4.9 %custom-call.7 = f32[1,64,64]{1,2,0:T(8,128)S(1)} custom-call(f32[1,64,64]{2,1,0:T(8,128)S(1)} %fusion.198), custom_call_target="InvertDiagBlocksLowerTriangular" | custom-call | tf_op jit(solution)/shard_map/jit(_solve_triangular)/triangular_solve | solution.py:31
  (155 shorter events, 50.4 us)
Async XLA Ops:
  0.0 20.5 %copy-start = (bf16[2,16,128,128]{3,2,1,0:T(8,128)(2,1)S(1)}, bf16[2,16,128,128]{3,2,1,0:T(8,128)(2,1)}, u32[]{:S(2)}) copy-start(bf16[2,16,128,128]{3,2,1,0:T(8,128)(2,1)} %param.12) | copy-start | bytes 3145732
  0.0 14.6 %copy-start.2 = (s32[2,32]{1,0:T(2,128)S(1)}, s32[2,32]{1,0:T(2,128)}, u32[]{:S(2)}) copy-start(s32[2,32]{1,0:T(2,128)} %param.13) | copy-start | bytes 772
  0.9 13.9 %collective-permute-start = (bf16[32,256]{1,0:T(8,128)(2,1)S(1)}, bf16[32,256]{1,0:T(8,128)(2,1)S(1)}, u32[]{:S(2)}, u32[]{:S(2)}) collective-permute-start(bf16[32,256]{1,0:T(8,128)(2,1)S(1)} %convert_element_type.183), channel_id=1, source_target_pairs={{0,12},{4,0},{8,4},{12,8},{1,13},{5,1},{9,5},{13,9},{2,14},{6,2},{... | collective-permute-start | bytes 49160 | tf_op jit(solution)/shard_map/ppermute | solution.py:59
  14.8 4.9 %collective-permute-start.1 = (bf16[32,512]{1,0:T(8,128)(2,1)S(1)}, bf16[32,512]{1,0:T(8,128)(2,1)S(1)}, u32[]{:S(2)}, u32[]{:S(2)}) collective-permute-start(bf16[32,512]{1,0:T(8,128)(2,1)S(1)} %pad_maximum_fusion), channel_id=1, source_target_pairs={{0,8},{4,12},{8,0},{12,4},{1,9},{5,13},{9,1},{13,5},{2,10},{6,14},... | collective-permute-start | bytes 98312 | tf_op jit(solution)/shard_map/ppermute | solution.py:59
  29.2 3.8 collective-permute-start.2
  33.0 4.8 %collective-permute-start.3 = (bf16[32,512]{1,0:T(8,128)(2,1)S(1)}, bf16[32,512]{1,0:T(8,128)(2,1)S(1)}, u32[]{:S(2)}, u32[]{:S(2)}) collective-permute-start(bf16[32,512]{1,0:T(8,128)(2,1)S(1)} %pad_maximum_fusion.1), channel_id=1, source_target_pairs={{0,8},{4,12},{8,0},{12,4},{1,9},{5,13},{9,1},{13,5},{2,10},{6,14},... | collective-permute-start | bytes 98312 | tf_op jit(solution)/shard_map/ppermute | solution.py:59
  38.6 7.8 %copy-start.1 = (f32[32,256]{1,0:T(8,128)S(1)}, f32[32,256]{1,0:T(8,128)}, u32[]{:S(2)}) copy-start(f32[32,256]{1,0:T(8,128)} %param.11) | copy-start | bytes 98308
  46.3 3.8 collective-permute-start.4
  50.1 4.8 %collective-permute-start.5 = (bf16[32,512]{1,0:T(8,128)(2,1)S(1)}, bf16[32,512]{1,0:T(8,128)(2,1)S(1)}, u32[]{:S(2)}, u32[]{:S(2)}) collective-permute-start(bf16[32,512]{1,0:T(8,128)(2,1)S(1)} %pad_maximum_fusion.2), channel_id=1, source_target_pairs={{0,8},{4,12},{8,0},{12,4},{1,9},{5,13},{9,1},{13,5},{2,10},{6,14},... | collective-permute-start | bytes 98312 | tf_op jit(solution)/shard_map/ppermute | solution.py:59
  64.6 5.4 %collective-permute-start.6 = (bf16[32,256]{1,0:T(8,128)(2,1)S(1)}, bf16[32,256]{1,0:T(8,128)(2,1)S(1)}, u32[]{:S(2)}, u32[]{:S(2)}) collective-permute-start(bf16[32,256]{1,0:T(8,128)(2,1)S(1)} %fusion.207), channel_id=1, source_target_pairs={{0,12},{4,0},{8,4},{12,8},{1,13},{5,1},{9,5},{13,9},{2,14},{6,2},{... | collective-permute-start | bytes 49160 | tf_op jit(solution)/shard_map/ppermute | solution.py:59
  70.0 5.0 %collective-permute-start.7 = (bf16[32,512]{1,0:T(8,128)(2,1)S(1)}, bf16[32,512]{1,0:T(8,128)(2,1)S(1)}, u32[]{:S(2)}, u32[]{:S(2)}) collective-permute-start(bf16[32,512]{1,0:T(8,128)(2,1)S(1)} %pad_maximum_fusion.3), channel_id=1, source_target_pairs={{0,8},{4,12},{8,0},{12,4},{1,9},{5,13},{9,1},{13,5},{2,10},{6,14},... | collective-permute-start | bytes 98312 | tf_op jit(solution)/shard_map/ppermute | solution.py:59
  83.3 5.7 %collective-permute-start.8 = (bf16[32,256]{1,0:T(8,128)(2,1)S(1)}, bf16[32,256]{1,0:T(8,128)(2,1)S(1)}, u32[]{:S(2)}, u32[]{:S(2)}) collective-permute-start(bf16[32,256]{1,0:T(8,128)(2,1)S(1)} %fusion.233), channel_id=1, source_target_pairs={{0,12},{4,0},{8,4},{12,8},{1,13},{5,1},{9,5},{13,9},{2,14},{6,2},{... | collective-permute-start | bytes 49160 | tf_op jit(solution)/shard_map/ppermute | solution.py:59
  89.0 4.8 %collective-permute-start.9 = (bf16[32,512]{1,0:T(8,128)(2,1)S(1)}, bf16[32,512]{1,0:T(8,128)(2,1)S(1)}, u32[]{:S(2)}, u32[]{:S(2)}) collective-permute-start(bf16[32,512]{1,0:T(8,128)(2,1)S(1)} %pad_maximum_fusion.4), channel_id=1, source_target_pairs={{0,8},{4,12},{8,0},{12,4},{1,9},{5,13},{9,1},{13,5},{2,10},{6,14},... | collective-permute-start | bytes 98312 | tf_op jit(solution)/shard_map/ppermute | solution.py:59
  103.5 5.6 %collective-permute-start.10 = (bf16[32,256]{1,0:T(8,128)(2,1)S(1)}, bf16[32,256]{1,0:T(8,128)(2,1)S(1)}, u32[]{:S(2)}, u32[]{:S(2)}) collective-permute-start(bf16[32,256]{1,0:T(8,128)(2,1)S(1)} %fusion.212), channel_id=1, source_target_pairs={{0,12},{4,0},{8,4},{12,8},{1,13},{5,1},{9,5},{13,9},{2,14},{6,2},{... | collective-permute-start | bytes 49160 | tf_op jit(solution)/shard_map/ppermute | solution.py:59
  109.1 4.8 %collective-permute-start.11 = (bf16[32,512]{1,0:T(8,128)(2,1)S(1)}, bf16[32,512]{1,0:T(8,128)(2,1)S(1)}, u32[]{:S(2)}, u32[]{:S(2)}) collective-permute-start(bf16[32,512]{1,0:T(8,128)(2,1)S(1)} %pad_maximum_fusion.5), channel_id=1, source_target_pairs={{0,8},{4,12},{8,0},{12,4},{1,9},{5,13},{9,1},{13,5},{2,10},{6,14},... | collective-permute-start | bytes 98312 | tf_op jit(solution)/shard_map/ppermute | solution.py:59
  122.3 5.6 %collective-permute-start.12 = (bf16[32,256]{1,0:T(8,128)(2,1)S(1)}, bf16[32,256]{1,0:T(8,128)(2,1)S(1)}, u32[]{:S(2)}, u32[]{:S(2)}) collective-permute-start(bf16[32,256]{1,0:T(8,128)(2,1)S(1)} %fusion.210), channel_id=1, source_target_pairs={{0,12},{4,0},{8,4},{12,8},{1,13},{5,1},{9,5},{13,9},{2,14},{6,2},{... | collective-permute-start | bytes 49160 | tf_op jit(solution)/shard_map/ppermute | solution.py:59
  127.9 4.8 %collective-permute-start.13 = (bf16[32,512]{1,0:T(8,128)(2,1)S(1)}, bf16[32,512]{1,0:T(8,128)(2,1)S(1)}, u32[]{:S(2)}, u32[]{:S(2)}) collective-permute-start(bf16[32,512]{1,0:T(8,128)(2,1)S(1)} %pad_maximum_fusion.6), channel_id=1, source_target_pairs={{0,8},{4,12},{8,0},{12,4},{1,9},{5,13},{9,1},{13,5},{2,10},{6,14},... | collective-permute-start | bytes 98312 | tf_op jit(solution)/shard_map/ppermute | solution.py:59
  142.3 5.6 %collective-permute-start.14 = (bf16[32,256]{1,0:T(8,128)(2,1)S(1)}, bf16[32,256]{1,0:T(8,128)(2,1)S(1)}, u32[]{:S(2)}, u32[]{:S(2)}) collective-permute-start(bf16[32,256]{1,0:T(8,128)(2,1)S(1)} %subtract_convert_fusion.3), channel_id=1, source_target_pairs={{0,12},{4,0},{8,4},{12,8},{1,13},{5,1},{9,5},{13,9},{2,14},{6,2},{... | collective-permute-start | bytes 49160 | tf_op jit(solution)/shard_map/ppermute | solution.py:59
  147.9 4.8 %collective-permute-start.15 = (bf16[32,512]{1,0:T(8,128)(2,1)S(1)}, bf16[32,512]{1,0:T(8,128)(2,1)S(1)}, u32[]{:S(2)}, u32[]{:S(2)}) collective-permute-start(bf16[32,512]{1,0:T(8,128)(2,1)S(1)} %pad_maximum_fusion.7), channel_id=1, source_target_pairs={{0,8},{4,12},{8,0},{12,4},{1,9},{5,13},{9,1},{13,5},{2,10},{6,14},... | collective-permute-start | bytes 98312 | tf_op jit(solution)/shard_map/ppermute | solution.py:59
  195.4 3.8 collective-permute-start.16
  199.2 4.8 %collective-permute-start.17 = (bf16[32,512]{1,0:T(8,128)(2,1)S(1)}, bf16[32,512]{1,0:T(8,128)(2,1)S(1)}, u32[]{:S(2)}, u32[]{:S(2)}) collective-permute-start(bf16[32,512]{1,0:T(8,128)(2,1)S(1)} %pad_maximum_fusion.8), channel_id=1, source_target_pairs={{0,8},{4,12},{8,0},{12,4},{1,9},{5,13},{9,1},{13,5},{2,10},{6,14},... | collective-permute-start | bytes 98312 | tf_op jit(solution)/shard_map/ppermute | solution.py:59
  213.6 3.8 collective-permute-start.18
  217.4 4.8 %collective-permute-start.19 = (bf16[32,512]{1,0:T(8,128)(2,1)S(1)}, bf16[32,512]{1,0:T(8,128)(2,1)S(1)}, u32[]{:S(2)}, u32[]{:S(2)}) collective-permute-start(bf16[32,512]{1,0:T(8,128)(2,1)S(1)} %pad_maximum_fusion.9), channel_id=1, source_target_pairs={{0,8},{4,12},{8,0},{12,4},{1,9},{5,13},{9,1},{13,5},{2,10},{6,14},... | collective-permute-start | bytes 98312 | tf_op jit(solution)/shard_map/ppermute | solution.py:59
  230.6 5.1 %collective-permute-start.20 = (bf16[32,256]{1,0:T(8,128)(2,1)S(1)}, bf16[32,256]{1,0:T(8,128)(2,1)S(1)}, u32[]{:S(2)}, u32[]{:S(2)}) collective-permute-start(bf16[32,256]{1,0:T(8,128)(2,1)S(1)} %fusion.232), channel_id=1, source_target_pairs={{0,12},{4,0},{8,4},{12,8},{1,13},{5,1},{9,5},{13,9},{2,14},{6,2},{... | collective-permute-start | bytes 49160 | tf_op jit(solution)/shard_map/ppermute | solution.py:59
  235.8 4.8 %collective-permute-start.21 = (bf16[32,512]{1,0:T(8,128)(2,1)S(1)}, bf16[32,512]{1,0:T(8,128)(2,1)S(1)}, u32[]{:S(2)}, u32[]{:S(2)}) collective-permute-start(bf16[32,512]{1,0:T(8,128)(2,1)S(1)} %pad_maximum_fusion.10), channel_id=1, source_target_pairs={{0,8},{4,12},{8,0},{12,4},{1,9},{5,13},{9,1},{13,5},{2,10},{6,14},... | collective-permute-start | bytes 98312 | tf_op jit(solution)/shard_map/ppermute | solution.py:59
  250.2 5.6 %collective-permute-start.22 = (bf16[32,256]{1,0:T(8,128)(2,1)S(1)}, bf16[32,256]{1,0:T(8,128)(2,1)S(1)}, u32[]{:S(2)}, u32[]{:S(2)}) collective-permute-start(bf16[32,256]{1,0:T(8,128)(2,1)S(1)} %fusion.208), channel_id=1, source_target_pairs={{0,12},{4,0},{8,4},{12,8},{1,13},{5,1},{9,5},{13,9},{2,14},{6,2},{... | collective-permute-start | bytes 49160 | tf_op jit(solution)/shard_map/ppermute | solution.py:59
  255.8 4.8 %collective-permute-start.23 = (bf16[32,512]{1,0:T(8,128)(2,1)S(1)}, bf16[32,512]{1,0:T(8,128)(2,1)S(1)}, u32[]{:S(2)}, u32[]{:S(2)}) collective-permute-start(bf16[32,512]{1,0:T(8,128)(2,1)S(1)} %pad_maximum_fusion.11), channel_id=1, source_target_pairs={{0,8},{4,12},{8,0},{12,4},{1,9},{5,13},{9,1},{13,5},{2,10},{6,14},... | collective-permute-start | bytes 98312 | tf_op jit(solution)/shard_map/ppermute | solution.py:59
  269.2 5.8 %collective-permute-start.24 = (bf16[32,256]{1,0:T(8,128)(2,1)S(1)}, bf16[32,256]{1,0:T(8,128)(2,1)S(1)}, u32[]{:S(2)}, u32[]{:S(2)}) collective-permute-start(bf16[32,256]{1,0:T(8,128)(2,1)S(1)} %fusion.211), channel_id=1, source_target_pairs={{0,12},{4,0},{8,4},{12,8},{1,13},{5,1},{9,5},{13,9},{2,14},{6,2},{... | collective-permute-start | bytes 49160 | tf_op jit(solution)/shard_map/ppermute | solution.py:59
  274.9 4.8 %collective-permute-start.25 = (bf16[32,512]{1,0:T(8,128)(2,1)S(1)}, bf16[32,512]{1,0:T(8,128)(2,1)S(1)}, u32[]{:S(2)}, u32[]{:S(2)}) collective-permute-start(bf16[32,512]{1,0:T(8,128)(2,1)S(1)} %pad_maximum_fusion.12), channel_id=1, source_target_pairs={{0,8},{4,12},{8,0},{12,4},{1,9},{5,13},{9,1},{13,5},{2,10},{6,14},... | collective-permute-start | bytes 98312 | tf_op jit(solution)/shard_map/ppermute | solution.py:59
  289.1 5.6 %collective-permute-start.26 = (bf16[32,256]{1,0:T(8,128)(2,1)S(1)}, bf16[32,256]{1,0:T(8,128)(2,1)S(1)}, u32[]{:S(2)}, u32[]{:S(2)}) collective-permute-start(bf16[32,256]{1,0:T(8,128)(2,1)S(1)} %fusion.213), channel_id=1, source_target_pairs={{0,12},{4,0},{8,4},{12,8},{1,13},{5,1},{9,5},{13,9},{2,14},{6,2},{... | collective-permute-start | bytes 49160 | tf_op jit(solution)/shard_map/ppermute | solution.py:59
  294.7 4.9 %collective-permute-start.27 = (bf16[32,512]{1,0:T(8,128)(2,1)S(1)}, bf16[32,512]{1,0:T(8,128)(2,1)S(1)}, u32[]{:S(2)}, u32[]{:S(2)}) collective-permute-start(bf16[32,512]{1,0:T(8,128)(2,1)S(1)} %pad_maximum_fusion.13), channel_id=1, source_target_pairs={{0,8},{4,12},{8,0},{12,4},{1,9},{5,13},{9,1},{13,5},{2,10},{6,14},... | collective-permute-start | bytes 98312 | tf_op jit(solution)/shard_map/ppermute | solution.py:59
  308.3 5.7 %collective-permute-start.28 = (bf16[32,256]{1,0:T(8,128)(2,1)S(1)}, bf16[32,256]{1,0:T(8,128)(2,1)S(1)}, u32[]{:S(2)}, u32[]{:S(2)}) collective-permute-start(bf16[32,256]{1,0:T(8,128)(2,1)S(1)} %fusion.214), channel_id=1, source_target_pairs={{0,12},{4,0},{8,4},{12,8},{1,13},{5,1},{9,5},{13,9},{2,14},{6,2},{... | collective-permute-start | bytes 49160 | tf_op jit(solution)/shard_map/ppermute | solution.py:59
  314.0 4.8 %collective-permute-start.29 = (bf16[32,512]{1,0:T(8,128)(2,1)S(1)}, bf16[32,512]{1,0:T(8,128)(2,1)S(1)}, u32[]{:S(2)}, u32[]{:S(2)}) collective-permute-start(bf16[32,512]{1,0:T(8,128)(2,1)S(1)} %pad_maximum_fusion.14), channel_id=1, source_target_pairs={{0,8},{4,12},{8,0},{12,4},{1,9},{5,13},{9,1},{13,5},{2,10},{6,14},... | collective-permute-start | bytes 98312 | tf_op jit(solution)/shard_map/ppermute | solution.py:59
  327.9 5.6 %collective-permute-start.30 = (bf16[32,256]{1,0:T(8,128)(2,1)S(1)}, bf16[32,256]{1,0:T(8,128)(2,1)S(1)}, u32[]{:S(2)}, u32[]{:S(2)}) collective-permute-start(bf16[32,256]{1,0:T(8,128)(2,1)S(1)} %subtract_convert_fusion.1), channel_id=1, source_target_pairs={{0,12},{4,0},{8,4},{12,8},{1,13},{5,1},{9,5},{13,9},{2,14},{6,2},{... | collective-permute-start | bytes 49160 | tf_op jit(solution)/shard_map/ppermute | solution.py:59
  333.5 4.8 %collective-permute-start.31 = (bf16[32,512]{1,0:T(8,128)(2,1)S(1)}, bf16[32,512]{1,0:T(8,128)(2,1)S(1)}, u32[]{:S(2)}, u32[]{:S(2)}) collective-permute-start(bf16[32,512]{1,0:T(8,128)(2,1)S(1)} %pad_maximum_fusion.15), channel_id=1, source_target_pairs={{0,8},{4,12},{8,0},{12,4},{1,9},{5,13},{9,1},{13,5},{2,10},{6,14},... | collective-permute-start | bytes 98312 | tf_op jit(solution)/shard_map/ppermute | solution.py:59
